TPU v7x, 32 devices: a whole 2x2x4 slice. The times are simulated.
32 devices in a mesh: group: 2 (over x), seq: 8 (over z, y), dp: 2 (over core).
Axes of the slice: x: 2, y: 2, z: 4, core: 2. Of those that a mesh axis runs over, the one named last changes fastest.
Arguments:
- queries: bfloat16 [4, 1024, 512], P(('group', 'dp'), 'seq'), parts along dimension 0, may hold values from -6 to 6
- key_rows: bfloat16 [4, 1024, 512], P(('group', 'dp'), 'seq'), parts along dimension 0, may hold values from -6 to 6
- value_rows: bfloat16 [4, 1024, 768], P(('group', 'dp'), 'seq'), parts along dimension 0, may hold values from -6 to 6
- trunk_state: bfloat16 [4, 1024, 768], P(('group', 'dp'), 'seq'), parts along dimension 0, may hold values from -6 to 6
- skip_input: bfloat16 [4, 2048, 768], P(('group', 'dp'), 'seq'), parts along dimension 0, may hold values from -6 to 6
- norm_gain: bfloat16 [768], replicated, may hold values from 0.099609375 to 1.8984375
- conv_weight: bfloat16 [3840, 384], replicated, may hold values from -0.09375 to 0.09375
- cotangent: bfloat16 [4, 2048, 384], P(('group', 'dp'), 'seq'), parts along dimension 0, may hold values from -6 to 6
Outputs:
- decoded: bfloat16 [4, 2048, 384], P(('group', 'dp'), 'seq'), parts along dimension 0
- grad_queries: bfloat16 [4, 1024, 512], P(('group', 'dp'), 'seq'), parts along dimension 0
- grad_keys: bfloat16 [4, 1024, 512], P(('group', 'dp'), 'seq'), parts along dimension 0
- grad_values: bfloat16 [4, 1024, 768], P(('group', 'dp'), 'seq'), parts along dimension 0
- grad_trunk: bfloat16 [4, 1024, 768], P(('group', 'dp'), 'seq'), parts along dimension 0
- grad_skip: bfloat16 [4, 2048, 768], P(('group', 'dp'), 'seq'), parts along dimension 0
- grad_weight: float32 [7680, 384], P(('group', 'seq', 'dp')), parts along dimension 0
There are 2 independent parts, one for each index of `group`. A program takes and returns all parts, laid end to end along the dimension named above; an argument that names none is the same for every part. Nothing has to cross between parts.
All inputs are finite; a program needn't handle non-finite values.
Results may differ from a plain program's by a relative error of at most 0.029.
Values may be sent and summed in bfloat16 or wider, within the bound.
No kernel may reach another device: no remote copies, remote signals or barrier semaphores. Data moves between devices by JAX's collectives and lax.ppermute only.
A program may use at most 128 MiB of HBM per device.

v0:
```python
import math
import jax
import jax.numpy as jnp
from jax import lax
from jax.sharding import PartitionSpec as P

H = 4
DK = 128
DV = 192
C = 768
CO = 384
KW = 5


def extended(array, sides, width):
    for axis, dim in sides:
        count, length = (lax.axis_size(axis), array.shape[dim])
        up = [(i, (i + 1) % count) for i in range(count - 1)]
        down = [(j, i) for i, j in up]
        last = lax.slice_in_dim(array, length - width, length, axis=dim)
        initial = lax.slice_in_dim(array, 0, width, axis=dim)
        before = lax.ppermute(last, axis, up)
        after = lax.ppermute(initial, axis, down)
        array = jnp.concatenate([before, array, after], axis=dim)
    return array


def gelu_parts(preact):
    cdf_value = 0.5 * (1.0 + jax.scipy.special.erf(preact * (1.0 / math.sqrt(2.0))))
    density = jnp.exp(-0.5 * preact * preact) * (1.0 / math.sqrt(2.0 * math.pi))
    return (preact * cdf_value, cdf_value + preact * density)


def window_rows(padded, kernel, row_count):
    return jnp.concatenate(
        [padded[offset : offset + row_count] for offset in range(kernel)], axis=1
    )


def body(queries, key_rows, value_rows, trunk_state, skip_input, norm_gain, conv_weight, cotangent):
    score_scale = DK ** (-0.5)
    local_tokens = queries.shape[1]
    positions = 2 * local_tokens
    half_kernel = KW // 2
    query_heads = queries[0].reshape(local_tokens, H, DK)
    gathered = (
        lax.all_gather(key_rows, "seq", axis=1, tiled=True),
        lax.all_gather(value_rows, "seq", axis=1, tiled=True),
    )
    all_keys = gathered[0][0].reshape(-1, H, DK)
    all_values = gathered[1][0].reshape(-1, H, DV)
    scores = (
        jnp.einsum("ihd,jhd->hij", query_heads, all_keys, preferred_element_type=jnp.float32)
        * score_scale
    )
    row_peak = jnp.max(scores, axis=2, keepdims=True)
    row_total = jnp.sum(jnp.exp(scores - row_peak), axis=2, keepdims=True)
    logsum = row_peak + jnp.log(row_total)
    softmax = jnp.exp(scores - logsum)
    rounded = softmax.astype(jnp.bfloat16)
    attended = jnp.einsum(
        "hij,jhd->ihd", rounded, all_values, preferred_element_type=jnp.float32
    ).astype(jnp.bfloat16)
    hidden = trunk_state[0].astype(jnp.float32) + attended.reshape(local_tokens, H * DV).astype(
        jnp.float32
    )
    merged = jnp.repeat(hidden, 2, axis=0) + skip_input[0].astype(jnp.float32)
    inverse = lax.rsqrt(jnp.mean(merged * merged, axis=1, keepdims=True) + 1e-06)
    channel_gain = norm_gain.astype(jnp.float32)
    normed = (merged * inverse * channel_gain).astype(jnp.bfloat16)
    padded = extended(normed, (("seq", 0),), half_kernel)
    columns = window_rows(padded, KW, positions)
    preact = jnp.dot(columns, conv_weight, preferred_element_type=jnp.float32)
    activated, derivative = gelu_parts(preact)
    decoded = activated.astype(jnp.bfloat16)
    grad_pre = (cotangent[0].astype(jnp.float32) * derivative).astype(jnp.bfloat16)
    grad_padded = extended(grad_pre, (("seq", 0),), half_kernel)
    norm_scale = (lax.axis_size("dp") * positions * lax.axis_size("seq")) ** (-0.5)
    grad_weight = lax.psum_scatter(
        lax.dot_general(
            columns, grad_pre, (((0,), (0,)), ((), ())), preferred_element_type=jnp.float32
        )
        * norm_scale,
        ("seq", "dp"),
        scatter_dimension=0,
        tiled=True,
    )
    stacked = jnp.stack(
        [
            grad_padded[2 * half_kernel - offset : 2 * half_kernel - offset + positions]
            for offset in range(KW)
        ],
        axis=1,
    )
    weight_blocks = conv_weight.reshape(KW, C, CO)
    grad_normed = jnp.einsum(
        "pko,kco->pc", stacked, weight_blocks, preferred_element_type=jnp.float32
    )
    scaled_grad = grad_normed * channel_gain
    grad_merged = inverse * scaled_grad - merged * inverse**3 * jnp.mean(
        scaled_grad * merged, axis=1, keepdims=True
    )
    grad_skip = grad_merged.astype(jnp.bfloat16)
    grad_trunk = grad_merged.reshape(local_tokens, 2, C).sum(axis=1).astype(jnp.bfloat16)
    grad_heads = grad_trunk.reshape(local_tokens, H, DV)
    row_delta = jnp.sum(grad_heads.astype(jnp.float32) * attended.astype(jnp.float32), axis=2)
    value_grad = jnp.einsum(
        "ihd,jhd->hij", grad_heads, all_values, preferred_element_type=jnp.float32
    )
    slopes = (softmax * (value_grad - row_delta.T[:, :, None])).astype(jnp.bfloat16)
    grad_queries = (
        jnp.einsum("hij,jhd->ihd", slopes, all_keys, preferred_element_type=jnp.float32)
        * score_scale
    ).astype(jnp.bfloat16)
    key_part = (
        jnp.einsum("hij,ihd->jhd", slopes, query_heads, preferred_element_type=jnp.float32)
        * score_scale
    )
    value_part = jnp.einsum("hij,ihd->jhd", rounded, grad_heads, preferred_element_type=jnp.float32)
    summed = lax.psum_scatter(
        jnp.concatenate(
            [
                key_part.reshape(lax.axis_size("seq") * local_tokens, H * DK),
                value_part.reshape(lax.axis_size("seq") * local_tokens, H * DV),
            ],
            axis=1,
        ).astype(jnp.bfloat16),
        "seq",
        scatter_dimension=0,
        tiled=True,
    ).astype(jnp.float32)
    grad_keys = summed[:, : H * DK].astype(jnp.bfloat16)
    grad_values = summed[:, H * DK :].astype(jnp.bfloat16)
    return (
        decoded[None],
        grad_queries.reshape(local_tokens, H * DK)[None],
        grad_keys[None],
        grad_values[None],
        grad_trunk[None],
        grad_skip[None],
        grad_weight,
    )


def solution(mesh):
    return jax.shard_map(
        body,
        mesh=mesh,
        in_specs=(
            P(("group", "dp"), "seq", None),
            P(("group", "dp"), "seq", None),
            P(("group", "dp"), "seq", None),
            P(("group", "dp"), "seq", None),
            P(("group", "dp"), "seq", None),
            P(),
            P(),
            P(("group", "dp"), "seq", None),
        ),
        out_specs=(
            P(("group", "dp"), "seq", None),
            P(("group", "dp"), "seq", None),
            P(("group", "dp"), "seq", None),
            P(("group", "dp"), "seq", None),
            P(("group", "dp"), "seq", None),
            P(("group", "dp"), "seq", None),
            P(("group", "seq", "dp"), None),
        ),
        check_vma=False,
    )
```

profile of v0, /device:TPU:0, one launch (start us, length us, event | category | flops | bytes accessed | tf_op | source)
XLA Modules:
  0.0 324.4 jit_solution(8928119127070148307)
XLA Ops:
  7.2 1.8 copy.24
  11.6 41.2 %all-gather.3.cloned.1.call-done = bf16[1,1024,512]{1,2,0:T(8,128)(2,1)} async-done(((bf16[1,128,512]{1,2,0:T(8,128)(2,1)}), bf16[1,1024,512]{1,2,0:T(8,128)(2,1)}) %all-gather.3.cloned.1.call-update) | async-done | bytes 1048592 | tf_op jit(solution)/shard_map/all_gather | solution.py:47
  52.8 1.8 multiply_reduce_fusion
  54.6 1.3 copy-done.1
  56.4 41.8 %all-gather.5.cloned.1.call-done = bf16[1,1024,768]{2,1,0:T(8,128)(2,1)} async-done(((bf16[1,128,768]{2,1,0:T(8,128)(2,1)}), bf16[1,1024,768]{2,1,0:T(8,128)(2,1)}) %all-gather.5.cloned.1.call-update) | async-done | bytes 1572880 | tf_op jit(solution)/shard_map/all_gather | solution.py:48
  98.2 2.6 copy.27
  100.8 2.8 fusion.2
  106.7 2.6 reshape.93
  109.2 2.6 broadcast_in_dim.26
  111.8 1.3 fusion.6
  113.2 1.3 multiply_convert_fusion.2
  114.5 2.6 collective-permute-start
  117.1 1.3 collective-permute-start.1
  118.6 4.3 %collective-permute-done.1 = bf16[2,768]{1,0:T(2,128)(2,1)S(1)} collective-permute-done((bf16[2,768]{1,0:T(2,128)(2,1)S(1)}, bf16[2,768]{1,0:T(2,128)(2,1)S(1)}, u32[]{:S(2)}, u32[]{:S(2)}) %collective-permute-start.1) | collective-permute-done | bytes 3104 | tf_op jit(solution)/shard_map/ppermute | solution.py:23
  123.1 2.0 fusion.16
  125.2 1.4 collective-permute-start.2
  126.6 5.4 %collective-permute-start.3 = (bf16[2,384]{1,0:T(2,128)(2,1)S(1)}, bf16[2,384]{1,0:T(2,128)(2,1)S(1)}, u32[]{:S(2)}, u32[]{:S(2)}) collective-permute-start(bf16[2,384]{1,0:T(2,128)(2,1)S(1)} %get-tuple-element.27), channel_id=1, source_target_pairs={{0,2},{2,4},{4,6},{6,8},{8,10},{10,12},{12,14},{1,3},{3,5},{5,7},{... | collective-permute-start | bytes 4616 | tf_op jit(solution)/shard_map/ppermute | solution.py:22
  134.6 1.3 convert_bitcast_fusion.1
  135.9 2.5 reshape.95
  138.4 2.8 reduce_sum.48
  141.2 1.7 copy.29
  144.1 3.6 %convolution_convert_fusion = bf16[4,192,1024]{2,1,0:T(8,128)(2,1)} fusion(bf16[128,4,192]{0,2,1:T(8,128)(2,1)} %bitcast.94, f32[4,128,1024]{2,1,0:T(8,128)} %copy-done.1, f32[4,128]{1,0:T(4,128)S(1)} %log_add_fusion), kind=kOutput, calls=%fused_computation.8 | convolution fusion | flops 203685888 | bytes 3868672 | tf_op jit(solution)/shard_map/hij,ihd->jhd/dot_general | solution.py:119
  149.6 1.4 multiply_convert_fusion
  151.0 2.3 copy.31
  153.2 2.6 copy.32
  155.9 3.4 %pad_maximum_fusion = bf16[1024,1280]{1,0:T(8,128)(2,1)} fusion(bf16[1024,768]{1,0:T(8,128)(2,1)} %copy.32, bf16[1024,512]{1,0:T(8,128)(2,1)} %copy.31), kind=kLoop, calls=%fused_computation.1 | loop fusion | flops 5242880 | bytes 5242880 | tf_op jit(solution)/shard_map/concatenate | solution.py:121
  159.3 5.3 %convolution_multiply_fusion = f32[3840,384]{1,0:T(8,128)} fusion(bf16[256,3840]{1,0:T(8,128)(2,1)} %copy-done.7, bf16[256,384]{1,0:T(8,128)(2,1)S(1)} %get-tuple-element.23), kind=kOutput, calls=%fused_computation | convolution fusion | flops 756449280 | bytes 8060928 | tf_op jit(solution)/shard_map/dot_general | solution.py:80
  164.7 2.0 fusion.3
  167.4 64.6 %reduce-scatter.3.cloned.1.call-done = bf16[128,1280]{1,0:T(8,128)(2,1)} async-done(((bf16[1024,1280]{1,0:T(8,128)(2,1)}), bf16[128,1280]{1,0:T(8,128)(2,1)}) %reduce-scatter.3.cloned.1.call-update) | async-done | bytes 327696 | tf_op jit(solution)/shard_map/reduce_scatter | solution.py:120
  232.0 1.6 slice_bitcast_fusion.1
  233.6 1.6 slice_bitcast_fusion
  235.2 82.7 %reduce-scatter.5.cloned.1.call-done = f32[240,384]{1,0:T(8,128)} async-done(((f32[3840,384]{1,0:T(8,128)}), f32[240,384]{1,0:T(8,128)}) %reduce-scatter.5.cloned.1.call-update) | async-done | bytes 368656 | tf_op jit(solution)/shard_map/reduce_scatter | solution.py:79
  (65 shorter events, 13.0 us)
Async XLA Ops:
  7.2 115.9 %copy-start = (bf16[3840,384]{1,0:T(8,128)(2,1)S(1)}, bf16[3840,384]{1,0:T(8,128)(2,1)}, u32[]{:S(2)}) copy-start(bf16[3840,384]{1,0:T(8,128)(2,1)} %param.14) | copy-start | bytes 8847364
  7.2 45.6 %all-gather.3.cloned.1.call-start = ((), (), s32[]{:S(2)}) async-start(), calls=%async_computation.2 | async-start | bytes 1179648 | tf_op jit(solution)/shard_map/all_gather | solution.py:47
  9.1 89.1 %all-gather.5.cloned.1.call-start = ((), (), s32[]{:S(2)}) async-start(), calls=%async_computation.3 | async-start | bytes 1769472 | tf_op jit(solution)/shard_map/all_gather | solution.py:48
  9.8 222.2 %reduce-scatter.3.cloned.1.call-start = ((), (), s32[]{:S(2)}) async-start(), calls=%async_computation.4 | async-start | bytes 2949120 | tf_op jit(solution)/shard_map/reduce_scatter | solution.py:120
  11.6 44.8 %copy-start.11 = (bf16[1,128,512]{1,2,0:T(8,128)(2,1)}, bf16[1,128,512]{1,2,0:T(8,128)(2,1)S(1)}, u32[]{:S(2)}) copy-start(bf16[1,128,512]{1,2,0:T(8,128)(2,1)S(1)} %copy.35) | copy-start | bytes 393220
  54.5 1.3 copy-start.1
  100.8 3.7 %copy-start.13 = (bf16[1,128,768]{2,1,0:T(8,128)(2,1)S(1)}, bf16[1,128,768]{2,1,0:T(8,128)(2,1)}, u32[]{:S(2)}) copy-start(bf16[1,128,768]{2,1,0:T(8,128)(2,1)} %param.11) | copy-start | bytes 589828
  103.5 0.9 copy-start.8
  105.5 6.3 %copy-start.6 = (bf16[1,256,768]{2,1,0:T(8,128)(2,1)S(1)}, bf16[1,256,768]{2,1,0:T(8,128)(2,1)}, u32[]{:S(2)}) copy-start(bf16[1,256,768]{2,1,0:T(8,128)(2,1)} %param.12) | copy-start | bytes 1179652
  114.4 8.7 %copy-start.14 = (bf16[1,256,384]{2,1,0:T(8,128)(2,1)S(1)}, bf16[1,256,384]{2,1,0:T(8,128)(2,1)}, u32[]{:S(2)}) copy-start(bf16[1,256,384]{2,1,0:T(8,128)(2,1)} %param.15) | copy-start | bytes 589828
  114.5 3.9 %collective-permute-start = (bf16[2,768]{1,0:T(2,128)(2,1)S(1)}, bf16[2,768]{1,0:T(2,128)(2,1)S(1)}, u32[]{:S(2)}, u32[]{:S(2)}) collective-permute-start(bf16[2,768]{1,0:T(2,128)(2,1)S(1)} %get-tuple-element.26), channel_id=1, source_target_pairs={{0,2},{2,4},{4,6},{6,8},{8,10},{10,12},{12,14},{1,3},{3,5},{5,7},{... | collective-permute-start | bytes 9224 | tf_op jit(solution)/shard_map/ppermute | solution.py:22
  117.1 5.8 %collective-permute-start.1 = (bf16[2,768]{1,0:T(2,128)(2,1)S(1)}, bf16[2,768]{1,0:T(2,128)(2,1)S(1)}, u32[]{:S(2)}, u32[]{:S(2)}) collective-permute-start(bf16[2,768]{1,0:T(2,128)(2,1)S(1)} %get-tuple-element.25), channel_id=1, source_target_pairs={{2,0},{4,2},{6,4},{8,6},{10,8},{12,10},{14,12},{3,1},{5,3},{7,5},{... | collective-permute-start | bytes 9224 | tf_op jit(solution)/shard_map/ppermute | solution.py:23
  123.1 2.0 copy-start.7
  125.1 8.3 %copy-start.4 = (f32[256,768]{1,0:T(8,128)S(1)}, f32[256,768]{1,0:T(8,128)}, u32[]{:S(2)}) copy-start(f32[256,768]{1,0:T(8,128)} %reshape.93) | copy-start | bytes 2359300
  125.2 6.9 %collective-permute-start.2 = (bf16[2,384]{1,0:T(2,128)(2,1)S(1)}, bf16[2,384]{1,0:T(2,128)(2,1)S(1)}, u32[]{:S(2)}, u32[]{:S(2)}) collective-permute-start(bf16[2,384]{1,0:T(2,128)(2,1)S(1)} %get-tuple-element.28), channel_id=1, source_target_pairs={{2,0},{4,2},{6,4},{8,6},{10,8},{12,10},{14,12},{3,1},{5,3},{7,5},{... | collective-permute-start | bytes 4616 | tf_op jit(solution)/shard_map/ppermute | solution.py:23
  126.6 6.7 %collective-permute-start.3 = (bf16[2,384]{1,0:T(2,128)(2,1)S(1)}, bf16[2,384]{1,0:T(2,128)(2,1)S(1)}, u32[]{:S(2)}, u32[]{:S(2)}) collective-permute-start(bf16[2,384]{1,0:T(2,128)(2,1)S(1)} %get-tuple-element.27), channel_id=1, source_target_pairs={{0,2},{2,4},{4,6},{6,8},{8,10},{10,12},{12,14},{1,3},{3,5},{5,7},{... | collective-permute-start | bytes 4616 | tf_op jit(solution)/shard_map/ppermute | solution.py:22
  135.9 7.0 %copy-start.9 = (f32[4,128,192]{1,2,0:T(8,128)S(1)}, f32[4,128,192]{1,2,0:T(8,128)}, u32[]{:S(2)}) copy-start(f32[4,128,192]{1,2,0:T(8,128)} %copy-done.8) | copy-start | bytes 1179652
  142.9 4.8 %copy-start.2 = (f32[4,128,1024]{2,1,0:T(8,128)S(1)}, f32[4,128,1024]{2,1,0:T(8,128)}, u32[]{:S(2)}) copy-start(f32[4,128,1024]{2,1,0:T(8,128)} %copy-done.1) | copy-start | bytes 6291460
  142.9 4.8 %copy-start.3 = (bf16[1,1024,768]{1,2,0:T(8,128)(2,1)S(1)}, bf16[1,1024,768]{1,2,0:T(8,128)(2,1)}, u32[]{:S(2)}) copy-start(bf16[1,1024,768]{1,2,0:T(8,128)(2,1)} %copy.27) | copy-start | bytes 4718596
  142.9 4.8 %copy-start.10 = (bf16[128,768]{0,1:T(8,128)(2,1)S(1)}, bf16[128,768]{0,1:T(8,128)(2,1)}, u32[]{:S(2)}) copy-start(bf16[128,768]{0,1:T(8,128)(2,1)} %copy.29) | copy-start | bytes 589828
  147.7 1.9 copy-start.12
  148.6 1.0 copy-start.5
  159.3 158.6 %reduce-scatter.5.cloned.1.call-start = ((), (), s32[]{:S(2)}) async-start(), calls=%async_computation.5 | async-start | bytes 6266880 | tf_op jit(solution)/shard_map/reduce_scatter | solution.py:79
Sparse Core Ops, SparseCore 0:
  10.6 42.1 all-gather.2
  54.9 43.1 all-gather.4
  159.4 72.5 reduce-scatter.2
  236.4 81.4 reduce-scatter.4
where the time goes:
time: 325 us; the launch traced here: 324 us
  waiting for transfers between devices  236 us (73%)
  local copies, waits for them, and re-layouts  28.3 us (9%)
  matrix products  20.8 us (6%)
  other arithmetic  14 us (4%)
  between operations  14 us (4%)
  starting transfers between devices  10.9 us (3%)
    reduce_scatter x1, waiting for transfers between devices, body(): lax.psum_scatter(lax.dot_general(columns, grad_pre, (((0,), (0,)), ((), (...  82.7 us
    reduce_scatter x1, waiting for transfers between devices, body(): lax.psum_scatter(jnp.concatenate([key_part.reshape(lax.axis_size('seq') *...  64.6 us
    all_gather x1, waiting for transfers between devices, body(): lax.all_gather(value_rows, 'seq', axis=1, tiled=True)  41.8 us
    all_gather x1, waiting for transfers between devices, body(): lax.all_gather(key_rows, 'seq', axis=1, tiled=True)  41.2 us
    ppermute x2, starting transfers between devices, extended(): before = lax.ppermute(last, axis, up)  8.03 us
  transfers between devices with their start and end apart: 8, of which 6 were waited for; matrix products, arithmetic and copies ran while one was open for 5% of the time, Pallas kernels for 0%

commit v1 on v0

--- a/solution.py
+++ b/solution.py
@@ -10,6 +10,22 @@
 C = 768
 CO = 384
 KW = 5
+
+
+def ring_gather(x, axis, dim):
+    ways, here, step = (lax.axis_size(axis), lax.axis_index(axis), x.shape[dim])
+    lengths = [n * ways if d == dim else n for d, n in enumerate(x.shape)]
+    full = lax.dynamic_update_slice_in_dim(jnp.zeros(lengths, x.dtype), x, here * step, axis=dim)
+    going_up = going_down = x
+    for far in range(1, ways // 2 + 1):
+        going_up = lax.ppermute(going_up, axis, [(d, (d + 1) % ways) for d in range(ways)])
+        full = lax.dynamic_update_slice_in_dim(full, going_up, (here - far) % ways * step, axis=dim)
+        if 2 * far < ways:
+            going_down = lax.ppermute(going_down, axis, [(d, (d - 1) % ways) for d in range(ways)])
+            full = lax.dynamic_update_slice_in_dim(
+                full, going_down, (here + far) % ways * step, axis=dim
+            )
+    return full
 
 
 def extended(array, sides, width):
@@ -45,7 +61,7 @@
     query_heads = queries[0].reshape(local_tokens, H, DK)
     gathered = (
         lax.all_gather(key_rows, "seq", axis=1, tiled=True),
-        lax.all_gather(value_rows, "seq", axis=1, tiled=True),
+        ring_gather(value_rows, "seq", 1),
     )
     all_keys = gathered[0][0].reshape(-1, H, DK)
     all_values = gathered[1][0].reshape(-1, H, DV)

time: 325 us -> 289 us (0.89)
  waiting for transfers between devices: 236 us -> 171 us
  starting transfers between devices: 10.9 us -> 26.4 us
  local copies, waits for them, and re-layouts: 28.3 us -> 40.2 us
    all_gather x1 -> x0, waiting for transfers between devices: 41.8 us -> none  [body(): lax.all_gather(value_rows, 'seq', axis=1, tiled=True)]
    all_gather x1, waiting for transfers between devices: 41.2 us -> 0.01 us  [body(): lax.all_gather(key_rows, 'seq', axis=1, tiled=True)]
    ppermute x0 -> x7, waiting for transfers between devices: none -> 20.3 us  [the longest x4 16.6 us: ring_gather(): lax.ppermute(going_up, axis, [(d, (d + 1) % ways) for d in range(ways)])]
    ppermute x0 -> x7, starting transfers between devices: none -> 17.4 us  [the longest x3 16.1 us: ring_gather(): lax.ppermute(going_down, axis, [(d, (d - 1) % ways) for d in range(ways)])]
    ppermute x0 -> x7, local copies, waits for them, and re-layouts: none -> 7.61 us  [the longest x4 4.34 us: ring_gather(): lax.ppermute(going_up, axis, [(d, (d + 1) % ways) for d in range(ways)])]
    dynamic_update_slice x0 -> x8, local copies, waits for them, and re-layouts: none -> 5.78 us  [the longest x4 2.91 us: ring_gather(): lax.dynamic_update_slice_in_dim(full, going_up, (here - far) % ways * ste...]
  transfers between devices with their start and end apart: 8 -> 14, of which waited for: 6 -> 7; matrix products, arithmetic and copies ran while one was open for 5% -> 10% of each run, Pallas kernels for 0% -> 0%
where the time goes in v1:
time: 289 us; the launch traced here: 288 us
  waiting for transfers between devices  171 us (59%)
  local copies, waits for them, and re-layouts  40.2 us (14%)
  starting transfers between devices  26.4 us (9%)
  matrix products  21.8 us (8%)
  between operations  14.1 us (5%)
  other arithmetic  14 us (5%)
    reduce_scatter x1, waiting for transfers between devices, body(): lax.psum_scatter(lax.dot_general(columns, grad_pre, (((0,), (0,)), ((), (...  82.8 us
    reduce_scatter x1, waiting for transfers between devices, body(): lax.psum_scatter(jnp.concatenate([key_part.reshape(lax.axis_size('seq') *...  63 us
    ppermute x4, waiting for transfers between devices, ring_gather(): lax.ppermute(going_up, axis, [(d, (d + 1) % ways) for d in range(ways)])  16.6 us
    ppermute x3, starting transfers between devices, ring_gather(): lax.ppermute(going_down, axis, [(d, (d - 1) % ways) for d in range(ways)])  16.1 us
    ppermute x2, starting transfers between devices, extended(): before = lax.ppermute(last, axis, up)  6.15 us
  transfers between devices with their start and end apart: 14, of which 7 were waited for; matrix products, arithmetic and copies ran while one was open for 10% of the time, Pallas kernels for 0%

profile of v1, /device:TPU:0, one launch (start us, length us, event | category | flops | bytes accessed | tf_op | source)
XLA Modules:
  0.0 287.5 jit_solution(3637251710829692601)
XLA Ops:
  7.2 1.8 copy.39
  9.1 6.1 %collective-permute-start.1 = (bf16[1,128,768]{2,1,0:T(8,128)(2,1)}, bf16[1,128,768]{2,1,0:T(8,128)(2,1)}, u32[]{:S(2)}, u32[]{:S(2)}) collective-permute-start(bf16[1,128,768]{2,1,0:T(8,128)(2,1)} %param.10), channel_id=1, source_target_pairs={{0,14},{2,0},{4,2},{6,4},{8,6},{10,8},{12,10},{14,12},{1,15},{3,1}... | collective-permute-start | bytes 589832 | tf_op jit(solution)/shard_map/ppermute | solution.py:24
  18.1 1.4 broadcast_in_dim.28
  21.3 4.8 %collective-permute-start.3 = (bf16[1,128,768]{2,1,0:T(8,128)(2,1)}, bf16[1,128,768]{2,1,0:T(8,128)(2,1)}, u32[]{:S(2)}, u32[]{:S(2)}) collective-permute-start(bf16[1,128,768]{2,1,0:T(8,128)(2,1)} %collective-permute-done.1), channel_id=1, source_target_pairs={{0,14},{2,0},{4,2},{6,4},{8,6},{10,8},{12,10},{14,12},{1,15},{3,1}... | collective-permute-start | bytes 589832 | tf_op jit(solution)/shard_map/ppermute | solution.py:24
  28.7 3.6 %collective-permute-done.3 = bf16[1,128,768]{2,1,0:T(8,128)(2,1)} collective-permute-done((bf16[1,128,768]{2,1,0:T(8,128)(2,1)}, bf16[1,128,768]{2,1,0:T(8,128)(2,1)}, u32[]{:S(2)}, u32[]{:S(2)}) %collective-permute-start.3) | collective-permute-done | bytes 196640 | tf_op jit(solution)/shard_map/ppermute | solution.py:24
  33.4 5.2 %collective-permute-start.5 = (bf16[1,128,768]{2,1,0:T(8,128)(2,1)}, bf16[1,128,768]{2,1,0:T(8,128)(2,1)}, u32[]{:S(2)}, u32[]{:S(2)}) collective-permute-start(bf16[1,128,768]{2,1,0:T(8,128)(2,1)} %collective-permute-done.3), channel_id=1, source_target_pairs={{0,14},{2,0},{4,2},{6,4},{8,6},{10,8},{12,10},{14,12},{1,15},{3,1}... | collective-permute-start | bytes 589832 | tf_op jit(solution)/shard_map/ppermute | solution.py:24
  41.3 8.8 %collective-permute-done.4 = bf16[1,128,768]{2,1,0:T(8,128)(2,1)} collective-permute-done((bf16[1,128,768]{2,1,0:T(8,128)(2,1)}, bf16[1,128,768]{2,1,0:T(8,128)(2,1)}, u32[]{:S(2)}, u32[]{:S(2)}) %collective-permute-start.4) | collective-permute-done | bytes 196640 | tf_op jit(solution)/shard_map/ppermute | solution.py:21
  54.8 7.8 %collective-permute-done.6 = bf16[1,128,768]{2,1,0:T(8,128)(2,1)} collective-permute-done((bf16[1,128,768]{2,1,0:T(8,128)(2,1)}, bf16[1,128,768]{2,1,0:T(8,128)(2,1)}, u32[]{:S(2)}, u32[]{:S(2)}) %collective-permute-start.6) | collective-permute-done | bytes 196640 | tf_op jit(solution)/shard_map/ppermute | solution.py:21
  64.5 1.8 multiply_reduce_fusion
  66.8 2.4 fusion.2
  72.3 2.6 reshape.93
  74.9 2.6 broadcast_in_dim.30
  80.1 1.4 collective-permute-start.7
  83.1 3.9 %collective-permute-done.8 = bf16[2,768]{1,0:T(2,128)(2,1)S(1)} collective-permute-done((bf16[2,768]{1,0:T(2,128)(2,1)S(1)}, bf16[2,768]{1,0:T(2,128)(2,1)S(1)}, u32[]{:S(2)}, u32[]{:S(2)}) %collective-permute-start.8) | collective-permute-done | bytes 3104 | tf_op jit(solution)/shard_map/ppermute | solution.py:39
  87.3 2.0 fusion.16
  89.3 1.4 collective-permute-start.9
  90.7 4.7 %collective-permute-start.10 = (bf16[2,384]{1,0:T(2,128)(2,1)S(1)}, bf16[2,384]{1,0:T(2,128)(2,1)S(1)}, u32[]{:S(2)}, u32[]{:S(2)}) collective-permute-start(bf16[2,384]{1,0:T(2,128)(2,1)S(1)} %get-tuple-element.27), channel_id=1, source_target_pairs={{0,2},{2,4},{4,6},{6,8},{8,10},{10,12},{12,14},{1,3},{3,5},{5,7},{... | collective-permute-start | bytes 4616 | tf_op jit(solution)/shard_map/ppermute | solution.py:38
  99.1 2.5 reshape.95
  101.6 2.8 reduce_sum.48
  104.4 1.7 copy.43
  107.3 3.5 %convolution_convert_fusion = bf16[4,192,1024]{2,1,0:T(8,128)(2,1)} fusion(bf16[128,4,192]{0,2,1:T(8,128)(2,1)} %bitcast.92, f32[4,128,1024]{2,1,0:T(8,128)} %copy-done.1, f32[4,128]{1,0:T(4,128)S(1)} %log_add_fusion), kind=kOutput, calls=%fused_computation.8 | convolution fusion | flops 203685888 | bytes 3868672 | tf_op jit(solution)/shard_map/hij,ihd->jhd/dot_general | solution.py:135
  110.8 2.3 multiply_convert_fusion.1
  114.1 1.4 multiply_convert_fusion
  115.5 2.3 copy.45
  117.8 2.6 copy.46
  120.4 3.4 %pad_maximum_fusion = bf16[1024,1280]{1,0:T(8,128)(2,1)} fusion(bf16[1024,768]{1,0:T(8,128)(2,1)} %copy.46, bf16[1024,512]{1,0:T(8,128)(2,1)} %copy.45), kind=kLoop, calls=%fused_computation.1 | loop fusion | flops 5242880 | bytes 5242880 | tf_op jit(solution)/shard_map/concatenate | solution.py:137
  123.9 5.3 %convolution_multiply_fusion = f32[3840,384]{1,0:T(8,128)} fusion(bf16[256,3840]{1,0:T(8,128)(2,1)} %copy-done.6, bf16[256,384]{1,0:T(8,128)(2,1)S(1)} %get-tuple-element.23), kind=kOutput, calls=%fused_computation | convolution fusion | flops 756449280 | bytes 8060928 | tf_op jit(solution)/shard_map/dot_general | solution.py:96
  129.2 2.0 fusion.3
  131.9 63.0 %reduce-scatter.3.cloned.1.call-done = bf16[128,1280]{1,0:T(8,128)(2,1)} async-done(((bf16[1024,1280]{1,0:T(8,128)(2,1)}), bf16[128,1280]{1,0:T(8,128)(2,1)}) %reduce-scatter.3.cloned.1.call-update) | async-done | bytes 327696 | tf_op jit(solution)/shard_map/reduce_scatter | solution.py:136
  195.0 1.6 slice_bitcast_fusion.1
  196.5 1.6 slice_bitcast_fusion
  198.2 82.8 %reduce-scatter.5.cloned.1.call-done = f32[240,384]{1,0:T(8,128)} async-done(((f32[3840,384]{1,0:T(8,128)}), f32[240,384]{1,0:T(8,128)}) %reduce-scatter.5.cloned.1.call-update) | async-done | bytes 368656 | tf_op jit(solution)/shard_map/reduce_scatter | solution.py:95
  (90 shorter events, 32.2 us)
Async XLA Ops:
  7.2 80.1 %copy-start = (bf16[3840,384]{1,0:T(8,128)(2,1)S(1)}, bf16[3840,384]{1,0:T(8,128)(2,1)}, u32[]{:S(2)}) copy-start(bf16[3840,384]{1,0:T(8,128)(2,1)} %param.14) | copy-start | bytes 8847364
  7.2 57.3 %all-gather.2.cloned.1.call-start = ((), (), s32[]{:S(2)}) async-start(), calls=%async_computation.2 | async-start | bytes 1179648 | tf_op jit(solution)/shard_map/all_gather | solution.py:63
  9.1 185.9 %reduce-scatter.3.cloned.1.call-start = ((), (), s32[]{:S(2)}) async-start(), calls=%async_computation.3 | async-start | bytes 2949120 | tf_op jit(solution)/shard_map/reduce_scatter | solution.py:136
  9.1 11.1 %collective-permute-start.1 = (bf16[1,128,768]{2,1,0:T(8,128)(2,1)}, bf16[1,128,768]{2,1,0:T(8,128)(2,1)}, u32[]{:S(2)}, u32[]{:S(2)}) collective-permute-start(bf16[1,128,768]{2,1,0:T(8,128)(2,1)} %param.10), channel_id=1, source_target_pairs={{0,14},{2,0},{4,2},{6,4},{8,6},{10,8},{12,10},{14,12},{1,15},{3,1}... | collective-permute-start | bytes 589832 | tf_op jit(solution)/shard_map/ppermute | solution.py:24
  15.2 10.9 %collective-permute-start = (bf16[1,128,768]{2,1,0:T(8,128)(2,1)}, bf16[1,128,768]{2,1,0:T(8,128)(2,1)}, u32[]{:S(2)}, u32[]{:S(2)}) collective-permute-start(bf16[1,128,768]{2,1,0:T(8,128)(2,1)} %param.10), channel_id=1, source_target_pairs={{0,2},{2,4},{4,6},{6,8},{8,10},{10,12},{12,14},{14,0},{1,3},{3,5},... | collective-permute-start | bytes 589832 | tf_op jit(solution)/shard_map/ppermute | solution.py:21
  18.1 46.4 %copy-start.10 = (bf16[1,128,512]{1,2,0:T(8,128)(2,1)}, bf16[1,128,512]{1,2,0:T(8,128)(2,1)S(1)}, u32[]{:S(2)}) copy-start(bf16[1,128,512]{1,2,0:T(8,128)(2,1)S(1)} %copy.49) | copy-start | bytes 393220
  21.3 11.0 %collective-permute-start.3 = (bf16[1,128,768]{2,1,0:T(8,128)(2,1)}, bf16[1,128,768]{2,1,0:T(8,128)(2,1)}, u32[]{:S(2)}, u32[]{:S(2)}) collective-permute-start(bf16[1,128,768]{2,1,0:T(8,128)(2,1)} %collective-permute-done.1), channel_id=1, source_target_pairs={{0,14},{2,0},{4,2},{6,4},{8,6},{10,8},{12,10},{14,12},{1,15},{3,1}... | collective-permute-start | bytes 589832 | tf_op jit(solution)/shard_map/ppermute | solution.py:24
  27.2 11.5 %collective-permute-start.2 = (bf16[1,128,768]{2,1,0:T(8,128)(2,1)}, bf16[1,128,768]{2,1,0:T(8,128)(2,1)}, u32[]{:S(2)}, u32[]{:S(2)}) collective-permute-start(bf16[1,128,768]{2,1,0:T(8,128)(2,1)} %collective-permute-done), channel_id=1, source_target_pairs={{0,2},{2,4},{4,6},{6,8},{8,10},{10,12},{12,14},{14,0},{1,3},{3,5},... | collective-permute-start | bytes 589832 | tf_op jit(solution)/shard_map/ppermute | solution.py:21
  33.4 18.8 %collective-permute-start.5 = (bf16[1,128,768]{2,1,0:T(8,128)(2,1)}, bf16[1,128,768]{2,1,0:T(8,128)(2,1)}, u32[]{:S(2)}, u32[]{:S(2)}) collective-permute-start(bf16[1,128,768]{2,1,0:T(8,128)(2,1)} %collective-permute-done.3), channel_id=1, source_target_pairs={{0,14},{2,0},{4,2},{6,4},{8,6},{10,8},{12,10},{14,12},{1,15},{3,1}... | collective-permute-start | bytes 589832 | tf_op jit(solution)/shard_map/ppermute | solution.py:24
  39.8 10.3 %collective-permute-start.4 = (bf16[1,128,768]{2,1,0:T(8,128)(2,1)}, bf16[1,128,768]{2,1,0:T(8,128)(2,1)}, u32[]{:S(2)}, u32[]{:S(2)}) collective-permute-start(bf16[1,128,768]{2,1,0:T(8,128)(2,1)} %collective-permute-done.2), channel_id=1, source_target_pairs={{0,2},{2,4},{4,6},{6,8},{8,10},{10,12},{12,14},{14,0},{1,3},{3,5},... | collective-permute-start | bytes 589832 | tf_op jit(solution)/shard_map/ppermute | solution.py:21
  51.1 11.5 %collective-permute-start.6 = (bf16[1,128,768]{2,1,0:T(8,128)(2,1)}, bf16[1,128,768]{2,1,0:T(8,128)(2,1)}, u32[]{:S(2)}, u32[]{:S(2)}) collective-permute-start(bf16[1,128,768]{2,1,0:T(8,128)(2,1)} %collective-permute-done.4), channel_id=1, source_target_pairs={{0,2},{2,4},{4,6},{6,8},{8,10},{10,12},{12,14},{14,0},{1,3},{3,5},... | collective-permute-start | bytes 589832 | tf_op jit(solution)/shard_map/ppermute | solution.py:21
  66.3 2.9 %copy-start.1 = (f32[4,128,1024]{2,1,0:T(8,128)}, f32[4,128,1024]{2,1,0:T(8,128)S(1)}, u32[]{:S(2)}) copy-start(f32[4,128,1024]{2,1,0:T(8,128)S(1)} %get-tuple-element.32) | copy-start | bytes 6291460
  66.8 3.3 %copy-start.12 = (bf16[1,128,768]{2,1,0:T(8,128)(2,1)S(1)}, bf16[1,128,768]{2,1,0:T(8,128)(2,1)}, u32[]{:S(2)}) copy-start(bf16[1,128,768]{2,1,0:T(8,128)(2,1)} %param.11) | copy-start | bytes 589828
  69.2 0.9 copy-start.7
  71.2 6.3 %copy-start.5 = (bf16[1,256,768]{2,1,0:T(8,128)(2,1)S(1)}, bf16[1,256,768]{2,1,0:T(8,128)(2,1)}, u32[]{:S(2)}) copy-start(bf16[1,256,768]{2,1,0:T(8,128)(2,1)} %param.12) | copy-start | bytes 1179652
  80.1 7.2 %copy-start.13 = (bf16[1,256,384]{2,1,0:T(8,128)(2,1)S(1)}, bf16[1,256,384]{2,1,0:T(8,128)(2,1)}, u32[]{:S(2)}) copy-start(bf16[1,256,384]{2,1,0:T(8,128)(2,1)} %param.15) | copy-start | bytes 589828
  80.1 2.7 collective-permute-start.7
  81.6 5.5 %collective-permute-start.8 = (bf16[2,768]{1,0:T(2,128)(2,1)S(1)}, bf16[2,768]{1,0:T(2,128)(2,1)S(1)}, u32[]{:S(2)}, u32[]{:S(2)}) collective-permute-start(bf16[2,768]{1,0:T(2,128)(2,1)S(1)} %get-tuple-element.25), channel_id=1, source_target_pairs={{2,0},{4,2},{6,4},{8,6},{10,8},{12,10},{14,12},{3,1},{5,3},{7,5},{... | collective-permute-start | bytes 9224 | tf_op jit(solution)/shard_map/ppermute | solution.py:39
  87.3 2.0 copy-start.6
  89.3 7.4 %copy-start.3 = (f32[256,768]{1,0:T(8,128)S(1)}, f32[256,768]{1,0:T(8,128)}, u32[]{:S(2)}) copy-start(f32[256,768]{1,0:T(8,128)} %reshape.93) | copy-start | bytes 2359300
  89.3 6.2 %collective-permute-start.9 = (bf16[2,384]{1,0:T(2,128)(2,1)S(1)}, bf16[2,384]{1,0:T(2,128)(2,1)S(1)}, u32[]{:S(2)}, u32[]{:S(2)}) collective-permute-start(bf16[2,384]{1,0:T(2,128)(2,1)S(1)} %get-tuple-element.28), channel_id=1, source_target_pairs={{2,0},{4,2},{6,4},{8,6},{10,8},{12,10},{14,12},{3,1},{5,3},{7,5},{... | collective-permute-start | bytes 4616 | tf_op jit(solution)/shard_map/ppermute | solution.py:39
  90.7 5.8 %collective-permute-start.10 = (bf16[2,384]{1,0:T(2,128)(2,1)S(1)}, bf16[2,384]{1,0:T(2,128)(2,1)S(1)}, u32[]{:S(2)}, u32[]{:S(2)}) collective-permute-start(bf16[2,384]{1,0:T(2,128)(2,1)S(1)} %get-tuple-element.27), channel_id=1, source_target_pairs={{0,2},{2,4},{4,6},{6,8},{8,10},{10,12},{12,14},{1,3},{3,5},{5,7},{... | collective-permute-start | bytes 4616 | tf_op jit(solution)/shard_map/ppermute | solution.py:38
  99.1 7.0 %copy-start.8 = (f32[4,192,128]{2,1,0:T(8,128)S(1)}, f32[4,192,128]{2,1,0:T(8,128)}, u32[]{:S(2)}) copy-start(f32[4,192,128]{2,1,0:T(8,128)} %copy-done.7) | copy-start | bytes 1179652
  106.1 4.7 %copy-start.2 = (f32[4,128,1024]{2,1,0:T(8,128)S(1)}, f32[4,128,1024]{2,1,0:T(8,128)}, u32[]{:S(2)}) copy-start(f32[4,128,1024]{2,1,0:T(8,128)} %copy-done.1) | copy-start | bytes 6291460
  106.1 4.7 %copy-start.9 = (bf16[128,768]{0,1:T(8,128)(2,1)S(1)}, bf16[128,768]{0,1:T(8,128)(2,1)}, u32[]{:S(2)}) copy-start(bf16[128,768]{0,1:T(8,128)(2,1)} %copy.43) | copy-start | bytes 589828
  110.8 3.3 %copy-start.11 = (bf16[1,128,512]{1,2,0:T(8,128)(2,1)S(1)}, bf16[1,128,512]{1,2,0:T(8,128)(2,1)}, u32[]{:S(2)}) copy-start(bf16[1,128,512]{1,2,0:T(8,128)(2,1)} %copy-done.10) | copy-start | bytes 393220
  113.1 1.0 copy-start.4
  123.8 157.2 %reduce-scatter.5.cloned.1.call-start = ((), (), s32[]{:S(2)}) async-start(), calls=%async_computation.4 | async-start | bytes 6266880 | tf_op jit(solution)/shard_map/reduce_scatter | solution.py:95
Sparse Core Ops, SparseCore 0:
  10.6 45.2 all-gather.1
  123.9 70.9 reduce-scatter.2
  199.5 81.4 reduce-scatter.4
